TPU v7x, 512 devices: a whole 4x8x8 slice. The times are simulated.
512 devices in a mesh: row: 16 (over y, x_lo), col: 16 (over z, core), ka: 2 (over x_hi).
Axes of the slice: x: 4 (x_hi: 2, x_lo: 2; x = x_hi * 2 + x_lo), y: 8, z: 8, core: 2. Of those that a mesh axis runs over, the one named last changes fastest.
Arguments:
- pair: bfloat16 [512, 512, 128], P('row', ('col', 'ka')), may hold values from -6 to 6
- pair_mask: int32 [512, 512], P('row', ('col', 'ka')), may hold values from 0 to 1, as said below
- w_in: bfloat16 [2, 128, 512], replicated, may hold values from -0.5 to 0.5
- w_gate: bfloat16 [2, 128, 128], replicated, may hold values from -0.5 to 0.5
- w_out: bfloat16 [2, 128, 128], replicated, may hold values from -0.5 to 0.5
Outputs:
- updated: bfloat16 [512, 512, 128], P('row', ('col', 'ka'))
Inputs may be any that keep to these rules, and one draw needn't show every extreme that they name: pair_mask[i, j] = v[i] v[j] for a per-token 0/1 validity v; within each aligned run of 16 tokens the real tokens come first and there is at least one.
All inputs are finite; a program needn't handle non-finite values.
Results may differ from a plain program's by a relative error of at most 0.014.
Values may be sent and summed in bfloat16 or wider, within the bound.
No kernel may reach another device: no remote copies, remote signals or barrier semaphores. Data moves between devices by JAX's collectives and lax.ppermute only.
A program may use at most 64 MiB of HBM per device.

v0:
```python
import jax
import jax.numpy as jnp
from jax import lax
from jax.sharding import PartitionSpec as P


def from_root(value, axis, source):
    kept = jnp.where(lax.axis_index(axis) == source, value, 0).astype(value.dtype)
    return lax.psum(kept, axis)


def layer_norm(value):
    mean = jnp.mean(value, axis=-1, keepdims=True)
    centred = value - mean
    var = jnp.mean(centred * centred, axis=-1, keepdims=True)
    return centred / jnp.sqrt(var + 1e-05)


def prepare(pair, valid, weight_in, weight_gate):
    normed = layer_norm(pair.astype(jnp.float32)).astype(jnp.bfloat16)
    proj = jnp.einsum("ijc,cd->ijd", normed, weight_in, preferred_element_type=jnp.float32)
    width = proj.shape[-1] // 4
    left = (jax.nn.sigmoid(proj[..., :width]) * proj[..., width : 2 * width] * valid).astype(
        jnp.bfloat16
    )
    right = (
        jax.nn.sigmoid(proj[..., 2 * width : 3 * width]) * proj[..., 3 * width :] * valid
    ).astype(jnp.bfloat16)
    gate = jax.nn.sigmoid(
        jnp.einsum("ijc,cd->ijd", normed, weight_gate, preferred_element_type=jnp.float32)
    )
    return (left, right, gate)


def finish(pair, tri, gate, weight_out):
    normed = layer_norm(tri).astype(jnp.bfloat16)
    proj = jnp.einsum("ijc,cd->ijd", normed, weight_out, preferred_element_type=jnp.float32)
    return (pair.astype(jnp.float32) + gate * proj).astype(jnp.bfloat16)


def on_device(pair, pair_mask, w_in, w_gate, w_out):
    valid = pair_mask.astype(jnp.float32)[..., None]
    left, right, gate = prepare(pair, valid, w_in[0], w_gate[0])
    left_rows, right_rows = (
        lax.all_gather(left, "col", axis=1, tiled=True),
        lax.all_gather(right, "col", axis=1, tiled=True),
    )
    right_diag = from_root(right_rows, "row", lax.axis_index("col"))
    partial_value = jnp.einsum(
        "ikc,jkc->ijc", left_rows, right_diag, preferred_element_type=jnp.float32
    )
    tri = lax.psum_scatter(
        partial_value.astype(jnp.bfloat16), "ka", scatter_dimension=1, tiled=True
    ).astype(jnp.float32)
    middle = finish(pair, tri, gate, w_out[0])
    left, right, gate = prepare(middle, valid, w_in[1], w_gate[1])
    left_cols, right_cols = (
        lax.all_gather(left, "row", axis=0, tiled=True),
        lax.all_gather(right, "row", axis=0, tiled=True),
    )
    left_wide = lax.all_gather(left_cols, "ka", axis=1, tiled=True)
    left_diag = from_root(left_wide, "col", lax.axis_index("row"))
    tri = jnp.einsum("kic,kjc->ijc", left_diag, right_cols, preferred_element_type=jnp.float32)
    return finish(middle, tri, gate, w_out[1])


def solution(mesh):
    placed = (P("row", ("col", "ka"), None), P("row", ("col", "ka")), P(), P(), P())
    return jax.shard_map(
        on_device,
        mesh=mesh,
        in_specs=placed,
        out_specs=P("row", ("col", "ka"), None),
        check_vma=False,
    )
```

profile of v0, /device:TPU:1, one launch (start us, length us, event | category | flops | bytes accessed | tf_op | source)
XLA Modules:
  0.0 666.7 jit_solution(9475400611187420991)
XLA Ops:
  6.5 1.0 convert_reduce_fusion.1
  7.7 1.1 fusion.18
  9.1 0.7 convert_element_type.56
  9.8 1.3 fusion.42
  11.2 0.9 fusion.31
  12.1 0.7 all-gather.8.cloned.1.call-update
  12.9 49.2 %all-gather.6.cloned.1.call-done = bf16[32,256,128]{2,1,0:T(8,128)(2,1)} async-done(((bf16[32,16,128]{2,1,0:T(8,128)(2,1)}), bf16[32,256,128]{2,1,0:T(8,128)(2,1)}) %all-gather.6.cloned.1.call-update) | async-done | bytes 2097168 | tf_op jit(solution)/shard_map/all_gather | solution.py:46
  62.0 1.4 broadcast_select_fusion.1
  63.6 43.2 %all-gather.8.cloned.1.call-done = bf16[32,256,128]{2,1,0:T(8,128)(2,1)} async-done(((bf16[32,16,128]{2,1,0:T(8,128)(2,1)}), bf16[32,256,128]{2,1,0:T(8,128)(2,1)}) %all-gather.8.cloned.1.call-update) | async-done | bytes 2097168 | tf_op jit(solution)/shard_map/all_gather | solution.py:45
  106.8 15.2 %copy.49 = bf16[32,256,128]{0,1,2:T(8,128)(2,1)} copy(bf16[32,256,128]{2,1,0:T(8,128)(2,1)} %all-gather.8.cloned.1.call-done) | data formatting | bytes 4194304 | tf_op jit(solution)/shard_map/all_gather | solution.py:45
  122.0 128.2 %all-reduce.3.cloned.1.call-done = bf16[32,256,128]{2,1,0:T(8,128)(2,1)} async-done(((bf16[32,256,128]{2,1,0:T(8,128)(2,1)}), bf16[32,256,128]{2,1,0:T(8,128)(2,1)}) %all-reduce.3.cloned.1.call-update) | async-done | bytes 2097168 | tf_op jit(solution)/shard_map/psum | solution.py:9
  250.2 3.4 copy.48
  253.6 5.8 fusion
  259.6 0.3 fusion.10
  259.9 37.9 %reduce-scatter.2.cloned.1.call-done = bf16[32,16,128]{0,1,2:T(8,128)(2,1)} async-done(((bf16[32,32,128]{0,1,2:T(8,128)(2,1)}), bf16[32,16,128]{0,1,2:T(8,128)(2,1)}) %reduce-scatter.2.cloned.1.call-update) | async-done | bytes 131088 | tf_op jit(solution)/shard_map/reduce_scatter | solution.py:52
  297.8 1.2 convert_reduce_fusion
  299.0 1.3 fusion.14
  300.3 1.2 fusion.15
  301.5 0.5 copy.50
  302.9 0.4 fusion.40
  303.2 0.9 fusion.21
  304.2 64.7 %all-gather.12.cloned.1.call-done = bf16[512,16,128]{2,1,0:T(8,128)(2,1)} async-done(((bf16[32,16,128]{2,1,0:T(8,128)(2,1)}), bf16[512,16,128]{2,1,0:T(8,128)(2,1)}) %all-gather.12.cloned.1.call-update) | async-done | bytes 2097168 | tf_op jit(solution)/shard_map/all_gather | solution.py:58
  368.9 5.0 copy.55
  374.0 0.7 all-gather.10.cloned.1.call-update
  374.7 74.4 %all-gather.14.cloned.1.call-done = bf16[512,32,128]{0,1,2:T(8,128)(2,1)} async-done(((bf16[512,16,128]{0,1,2:T(8,128)(2,1)}), bf16[512,32,128]{0,1,2:T(8,128)(2,1)}) %all-gather.14.cloned.1.call-update) | async-done | bytes 4194320 | tf_op jit(solution)/shard_map/all_gather | solution.py:61
  449.1 2.2 broadcast_select_fusion
  451.7 64.2 %all-gather.10.cloned.1.call-done = bf16[512,16,128]{2,1,0:T(8,128)(2,1)} async-done(((bf16[32,16,128]{2,1,0:T(8,128)(2,1)}), bf16[512,16,128]{2,1,0:T(8,128)(2,1)}) %all-gather.10.cloned.1.call-update) | async-done | bytes 2097168 | tf_op jit(solution)/shard_map/all_gather | solution.py:59
  515.8 3.9 copy.56
  519.8 135.0 %all-reduce.5.cloned.1.call-done = bf16[512,32,128]{0,1,2:T(8,128)(2,1)} async-done(((bf16[512,32,128]{0,1,2:T(8,128)(2,1)}), bf16[512,32,128]{0,1,2:T(8,128)(2,1)}) %all-reduce.5.cloned.1.call-update) | async-done | bytes 4194320 | tf_op jit(solution)/shard_map/psum | solution.py:9
  654.8 3.4 fusion.57
  658.5 0.5 copy.57
  659.0 0.8 fusion.13
  (44 shorter events, 2.3 us)
Async XLA Ops:
  6.5 55.5 %all-gather.6.cloned.1.call-start = ((), (), s32[]{:S(2)}) async-start(), calls=%async_computation.1 | async-start | bytes 2228224 | tf_op jit(solution)/shard_map/all_gather | solution.py:46
  12.1 94.7 %all-gather.8.cloned.1.call-start = ((), (), s32[]{:S(2)}) async-start(), calls=%async_computation.3 | async-start | bytes 2228224 | tf_op jit(solution)/shard_map/all_gather | solution.py:45
  12.8 237.4 %all-reduce.3.cloned.1.call-start = ((), (), s32[]{:S(2)}) async-start(), calls=%async_computation.2 | async-start | bytes 4194304 | tf_op jit(solution)/shard_map/psum | solution.py:9
  63.5 234.3 %reduce-scatter.2.cloned.1.call-start = ((), (), s32[]{:S(2)}) async-start(), calls=%async_computation.4 | async-start | bytes 1572864 | tf_op jit(solution)/shard_map/reduce_scatter | solution.py:52
  253.6 5.9 copy-start
  253.6 5.9 copy-start.3
  259.5 42.5 %copy-start.2 = (bf16[2,128,128]{2,1,0:T(8,128)(2,1)S(1)}, bf16[2,128,128]{2,1,0:T(8,128)(2,1)}, u32[]{:S(2)}) copy-start(bf16[2,128,128]{2,1,0:T(8,128)(2,1)} %param.9) | copy-start | bytes 196612
  259.5 109.4 %all-gather.12.cloned.1.call-start = ((), (), s32[]{:S(2)}) async-start(), calls=%async_computation.6 | async-start | bytes 2228224 | tf_op jit(solution)/shard_map/all_gather | solution.py:58
  259.9 43.0 %copy-start.1 = (bf16[2,128,512]{2,1,0:T(8,128)(2,1)S(1)}, bf16[2,128,512]{2,1,0:T(8,128)(2,1)}, u32[]{:S(2)}) copy-start(bf16[2,128,512]{2,1,0:T(8,128)(2,1)} %param.7) | copy-start | bytes 786436
  304.1 145.0 %all-gather.14.cloned.1.call-start = ((), (), s32[]{:S(2)}) async-start(), calls=%async_computation.7 | async-start | bytes 6291456 | tf_op jit(solution)/shard_map/all_gather | solution.py:61
  373.9 141.9 %all-gather.10.cloned.1.call-start = ((), (), s32[]{:S(2)}) async-start(), calls=%async_computation.5 | async-start | bytes 2228224 | tf_op jit(solution)/shard_map/all_gather | solution.py:59
  374.7 280.1 %all-reduce.5.cloned.1.call-start = ((), (), s32[]{:S(2)}) async-start(), calls=%async_computation.8 | async-start | bytes 8388608 | tf_op jit(solution)/shard_map/psum | solution.py:9
Sparse Core Ops, SparseCore 0:
  12.2 49.8 all-gather.5
  64.1 42.6 all-gather.7
  109.7 140.4 all-reduce.2
  259.6 38.2 reduce-scatter.1
  304.2 64.6 all-gather.11
  374.0 75.0 all-gather.13
  451.2 64.6 all-gather.9
  518.2 136.5 all-reduce.4
where the time goes:
time: 667 us
  waiting for transfers between devices  598 us (90%)
  local copies, waits for them, and re-layouts  29.2 us (4%)
  between operations  13.7 us (2%)
  matrix products  12.7 us (2%)
  other arithmetic  12.5 us (2%)
    psum x2, waiting for transfers between devices, from_root(): return lax.psum(kept, axis)  263 us
    all_gather x1, waiting for transfers between devices, on_device(): left_wide = lax.all_gather(left_cols, 'ka', axis=1, tiled=True)  74.4 us
    all_gather x1, waiting for transfers between devices, on_device(): lax.all_gather(left, 'row', axis=0, tiled=True)  64.7 us
    all_gather x1, waiting for transfers between devices, on_device(): lax.all_gather(right, 'row', axis=0, tiled=True)  64.2 us
    all_gather x1, waiting for transfers between devices, on_device(): lax.all_gather(right, 'col', axis=1, tiled=True)  49.2 us
    all_gather x1, waiting for transfers between devices, on_device(): lax.all_gather(left, 'col', axis=1, tiled=True)  43.2 us
    reduce_scatter x1, waiting for transfers between devices, on_device(): lax.psum_scatter(partial_value.astype(jnp.bfloat16), 'ka', scatter_dimens...  37.9 us
    all_gather x1, local copies, waits for them, and re-layouts, on_device(): lax.all_gather(left, 'col', axis=1, tiled=True)  15.2 us
  transfers between devices with their start and end apart: 8, of which 8 were waited for; matrix products, arithmetic and copies ran while one was open for 4% of the time, Pallas kernels for 0%

commit v1 on v0

--- a/solution.py
+++ b/solution.py
@@ -2,6 +2,33 @@
 import jax.numpy as jnp
 from jax import lax
 from jax.sharding import PartitionSpec as P
+
+
+def watch_positions_on(own_rows, axis_k):
+    step_out = list(own_rows.shape[1:])
+    step_out[axis_k] *= own_rows.shape[0]
+    extra = jnp.moveaxis(own_rows, 0, axis_k).reshape(step_out)
+    return extra
+
+
+def _note_area(mine, shard_axis, on_dim=1):
+    n_blocks = lax.axis_size(shard_axis)
+    column = [(dev, (dev + 1) % n_blocks) for dev in range(n_blocks)]
+    vals = [(no, tick) for tick, no in column]
+    carry, y2 = ([], [])
+    for dev_j in range(n_blocks - 1):
+        if dev_j % 2 == 0:
+            tile_out = lax.ppermute(carry[-1] if carry else mine, shard_axis, column)
+            carry.append(tile_out)
+        else:
+            y2.append(lax.ppermute(y2[-1] if y2 else mine, shard_axis, vals))
+    oldest = jnp.stack([*carry[::-1], mine, *y2], 0)
+    wide_out = lax.axis_index(shard_axis)
+    small = len(carry)
+    high = wide_out - small
+    oldest = oldest[(jnp.arange(n_blocks) - high) % n_blocks]
+    r2 = watch_positions_on(oldest, on_dim)
+    return r2
 
 
 def from_root(value, axis, source):
@@ -43,7 +70,7 @@
     left, right, gate = prepare(pair, valid, w_in[0], w_gate[0])
     left_rows, right_rows = (
         lax.all_gather(left, "col", axis=1, tiled=True),
-        lax.all_gather(right, "col", axis=1, tiled=True),
+        _note_area(right, "col"),
     )
     right_diag = from_root(right_rows, "row", lax.axis_index("col"))
     partial_value = jnp.einsum(

time: 667 us -> 564 us (0.85)
  waiting for transfers between devices: 598 us -> 444 us
  starting transfers between devices: 0.29 us -> 36.5 us
  local copies, waits for them, and re-layouts: 29.2 us -> 42.4 us
    psum x2, waiting for transfers between devices: 263 us -> 172 us  [from_root(): return lax.psum(kept, axis)]
    all_gather x1 -> x0, waiting for transfers between devices: 49.2 us -> none  [on_device(): lax.all_gather(right, 'col', axis=1, tiled=True)]
    ppermute x0 -> x15, starting transfers between devices: none -> 36.2 us  [the longest x7 32.5 us: _note_area(): y2.append(lax.ppermute(y2[-1] if y2 else mine, shard_axis, vals))]
    all_gather x1, waiting for transfers between devices: 43.2 us -> 20 us  [on_device(): lax.all_gather(left, 'col', axis=1, tiled=True)]
    ppermute x0 -> x15, waiting for transfers between devices: none -> 10.8 us  [the longest x8 9.89 us: _note_area(): tile_out = lax.ppermute(carry[-1] if carry else mine, shard_axis, column)]
    unnamed x8 -> x23, local copies, waits for them, and re-layouts: 0.03 us -> 9.86 us
  transfers between devices with their start and end apart: 8 -> 22, of which waited for: 8 -> 21; matrix products, arithmetic and copies ran while one was open for 4% -> 7% of each run, Pallas kernels for 0% -> 0%
where the time goes in v1:
time: 564 us; the launch traced here: 563 us
  waiting for transfers between devices  444 us (79%)
  local copies, waits for them, and re-layouts  42.4 us (8%)
  starting transfers between devices  36.5 us (6%)
  between operations  15.3 us (3%)
  matrix products  13.2 us (2%)
  other arithmetic  11.3 us (2%)
    psum x2, waiting for transfers between devices, from_root(): return lax.psum(kept, axis)  172 us
    all_gather x1, waiting for transfers between devices, on_device(): left_wide = lax.all_gather(left_cols, 'ka', axis=1, tiled=True)  74.2 us
    all_gather x1, waiting for transfers between devices, on_device(): lax.all_gather(left, 'row', axis=0, tiled=True)  64.4 us
    all_gather x1, waiting for transfers between devices, on_device(): lax.all_gather(right, 'row', axis=0, tiled=True)  64.4 us
    reduce_scatter x1, waiting for transfers between devices, on_device(): lax.psum_scatter(partial_value.astype(jnp.bfloat16), 'ka', scatter_dimens...  37.8 us
    ppermute x7, starting transfers between devices, _note_area(): y2.append(lax.ppermute(y2[-1] if y2 else mine, shard_axis, vals))  32.5 us
    all_gather x1, waiting for transfers between devices, on_device(): lax.all_gather(left, 'col', axis=1, tiled=True)  20 us
    all_gather x1, local copies, waits for them, and re-layouts, on_device(): lax.all_gather(left, 'col', axis=1, tiled=True)  15.2 us
  transfers between devices with their start and end apart: 22, of which 21 were waited for; matrix products, arithmetic and copies ran while one was open for 7% of the time, Pallas kernels for 0%

profile of v1, /device:TPU:1, one launch (start us, length us, event | category | flops | bytes accessed | tf_op | source)
XLA Modules:
  0.0 563.0 jit_solution(11387668872643815256)
XLA Ops:
  7.4 1.0 convert_reduce_fusion.1
  8.6 1.1 fusion.18
  10.7 1.3 fusion.42
  12.8 3.5 collective-permute-start
  16.3 4.2 collective-permute-done
  20.7 4.8 collective-permute-start.8
  25.5 0.8 collective-permute-done.1
  26.4 4.6 collective-permute-start.9
  32.0 4.6 collective-permute-start.10
  37.7 4.6 collective-permute-start.11
  43.3 4.6 collective-permute-start.12
  48.9 4.7 collective-permute-start.13
  54.6 4.6 collective-permute-start.14
  70.4 2.5 gather_fusion
  73.7 3.0 copy.62
  76.8 20.0 %all-gather.5.cloned.1.call-done = bf16[32,256,128]{2,1,0:T(8,128)(2,1)} async-done(((bf16[32,16,128]{2,1,0:T(8,128)(2,1)}), bf16[32,256,128]{2,1,0:T(8,128)(2,1)}) %all-gather.5.cloned.1.call-update) | async-done | bytes 2097168 | tf_op jit(solution)/shard_map/all_gather | solution.py:72
  96.8 15.2 %copy.63 = bf16[32,256,128]{0,1,2:T(8,128)(2,1)} copy(bf16[32,256,128]{2,1,0:T(8,128)(2,1)} %all-gather.5.cloned.1.call-done) | data formatting | bytes 4194304 | tf_op jit(solution)/shard_map/all_gather | solution.py:72
  112.0 109.7 %all-reduce.3.cloned.1.call-done = bf16[32,256,128]{1,0,2:T(8,128)(2,1)} async-done(((bf16[32,256,128]{1,0,2:T(8,128)(2,1)}), bf16[32,256,128]{1,0,2:T(8,128)(2,1)}) %all-reduce.3.cloned.1.call-update) | async-done | bytes 2097168 | tf_op jit(solution)/shard_map/psum | solution.py:36
  221.7 6.4 %fusion = bf16[32,32,128]{0,1,2:T(8,128)(2,1)} fusion(bf16[32,256,128]{1,0,2:T(8,128)(2,1)} %all-reduce.3.cloned.1.call-done, bf16[32,256,128]{0,1,2:T(8,128)(2,1)} %copy.63), kind=kOutput, calls=%fused_computation.4 | convolution fusion | flops 67239936 | bytes 4456448 | tf_op jit(solution)/shard_map/ikc,jkc->ijc/dot_general | solution.py:76
  228.6 37.8 %reduce-scatter.2.cloned.1.call-done = bf16[32,16,128]{0,1,2:T(8,128)(2,1)} async-done(((bf16[32,32,128]{0,1,2:T(8,128)(2,1)}), bf16[32,16,128]{0,1,2:T(8,128)(2,1)}) %reduce-scatter.2.cloned.1.call-update) | async-done | bytes 131088 | tf_op jit(solution)/shard_map/reduce_scatter | solution.py:79
  266.3 1.2 convert_reduce_fusion
  267.6 1.3 fusion.14
  268.8 1.2 fusion.15
  271.7 0.9 fusion.21
  272.7 64.4 %all-gather.9.cloned.1.call-done = bf16[512,16,128]{2,1,0:T(8,128)(2,1)} async-done(((bf16[32,16,128]{2,1,0:T(8,128)(2,1)}), bf16[512,16,128]{2,1,0:T(8,128)(2,1)}) %all-gather.9.cloned.1.call-update) | async-done | bytes 2097168 | tf_op jit(solution)/shard_map/all_gather | solution.py:85
  337.1 4.9 copy.69
  342.9 74.2 %all-gather.11.cloned.1.call-done = bf16[512,32,128]{0,1,2:T(8,128)(2,1)} async-done(((bf16[512,16,128]{0,1,2:T(8,128)(2,1)}), bf16[512,32,128]{0,1,2:T(8,128)(2,1)}) %all-gather.11.cloned.1.call-update) | async-done | bytes 4194320 | tf_op jit(solution)/shard_map/all_gather | solution.py:88
  417.1 2.2 broadcast_select_fusion
  419.7 64.4 %all-gather.7.cloned.1.call-done = bf16[512,16,128]{2,1,0:T(8,128)(2,1)} async-done(((bf16[32,16,128]{2,1,0:T(8,128)(2,1)}), bf16[512,16,128]{2,1,0:T(8,128)(2,1)}) %all-gather.7.cloned.1.call-update) | async-done | bytes 2097168 | tf_op jit(solution)/shard_map/all_gather | solution.py:86
  484.1 3.9 copy.70
  488.1 62.3 %all-reduce.5.cloned.1.call-done = bf16[512,32,128]{0,1,2:T(8,128)(2,1)} async-done(((bf16[512,32,128]{0,1,2:T(8,128)(2,1)}), bf16[512,32,128]{0,1,2:T(8,128)(2,1)}) %all-reduce.5.cloned.1.call-update) | async-done | bytes 4194320 | tf_op jit(solution)/shard_map/psum | solution.py:36
  550.3 3.4 fusion.59
  (91 shorter events, 24.2 us)
Async XLA Ops:
  7.4 89.4 %all-gather.5.cloned.1.call-start = ((), (), s32[]{:S(2)}) async-start(), calls=%async_computation.2 | async-start | bytes 2228224 | tf_op jit(solution)/shard_map/all_gather | solution.py:72
  12.8 7.7 %collective-permute-start = (bf16[32,16,128]{2,1,0:T(8,128)(2,1)S(1)}, bf16[32,16,128]{2,1,0:T(8,128)(2,1)S(1)}, u32[]{:S(2)}, u32[]{:S(2)}) collective-permute-start(bf16[32,16,128]{2,1,0:T(8,128)(2,1)S(1)} %get-tuple-element.8), channel_id=1, source_target_pairs={{0,2},{2,4},{4,6},{6,8},{8,10},{10,12},{12,14},{14,16},{16,18},{18... | collective-permute-start | bytes 393224 | tf_op jit(solution)/shard_map/ppermute | solution.py:21
  20.5 5.8 %collective-permute-start.1 = (bf16[32,16,128]{2,1,0:T(8,128)(2,1)S(1)}, bf16[32,16,128]{2,1,0:T(8,128)(2,1)S(1)}, u32[]{:S(2)}, u32[]{:S(2)}) collective-permute-start(bf16[32,16,128]{2,1,0:T(8,128)(2,1)S(1)} %collective-permute-done), channel_id=1, source_target_pairs={{0,2},{2,4},{4,6},{6,8},{8,10},{10,12},{12,14},{14,16},{16,18},{18... | collective-permute-start | bytes 393224 | tf_op jit(solution)/shard_map/ppermute | solution.py:21
  20.7 5.7 %collective-permute-start.8 = (bf16[32,16,128]{2,1,0:T(8,128)(2,1)S(1)}, bf16[32,16,128]{2,1,0:T(8,128)(2,1)S(1)}, u32[]{:S(2)}, u32[]{:S(2)}) collective-permute-start(bf16[32,16,128]{2,1,0:T(8,128)(2,1)S(1)} %get-tuple-element.8), channel_id=1, source_target_pairs={{2,0},{4,2},{6,4},{8,6},{10,8},{12,10},{14,12},{16,14},{18,16},{20... | collective-permute-start | bytes 393224 | tf_op jit(solution)/shard_map/ppermute | solution.py:24
  26.3 5.6 collective-permute-start.2
  26.4 5.6 collective-permute-start.9
  31.9 5.6 collective-permute-start.3
  32.0 5.6 collective-permute-start.10
  37.5 5.6 collective-permute-start.4
  37.7 5.6 collective-permute-start.11
  43.1 5.6 collective-permute-start.5
  43.3 5.6 collective-permute-start.12
  48.7 5.6 collective-permute-start.6
  48.7 173.0 %all-reduce.3.cloned.1.call-start = ((), (), s32[]{:S(2)}) async-start(), calls=%async_computation.1 | async-start | bytes 4194304 | tf_op jit(solution)/shard_map/psum | solution.py:36
  48.9 5.7 %collective-permute-start.13 = (bf16[32,16,128]{2,1,0:T(8,128)(2,1)S(1)}, bf16[32,16,128]{2,1,0:T(8,128)(2,1)S(1)}, u32[]{:S(2)}, u32[]{:S(2)}) collective-permute-start(bf16[32,16,128]{2,1,0:T(8,128)(2,1)S(1)} %collective-permute-done.12), channel_id=1, source_target_pairs={{2,0},{4,2},{6,4},{8,6},{10,8},{12,10},{14,12},{16,14},{18,16},{20... | collective-permute-start | bytes 393224 | tf_op jit(solution)/shard_map/ppermute | solution.py:24
  54.3 5.6 collective-permute-start.7
  54.6 15.2 %collective-permute-start.14 = (bf16[32,16,128]{2,1,0:T(8,128)(2,1)S(1)}, bf16[32,16,128]{2,1,0:T(8,128)(2,1)S(1)}, u32[]{:S(2)}, u32[]{:S(2)}) collective-permute-start(bf16[32,16,128]{2,1,0:T(8,128)(2,1)S(1)} %collective-permute-done.13), channel_id=1, source_target_pairs={{2,0},{4,2},{6,4},{8,6},{10,8},{12,10},{14,12},{16,14},{18,16},{20... | collective-permute-start | bytes 393224 | tf_op jit(solution)/shard_map/ppermute | solution.py:24
  76.7 189.6 %reduce-scatter.2.cloned.1.call-start = ((), (), s32[]{:S(2)}) async-start(), calls=%async_computation.3 | async-start | bytes 1572864 | tf_op jit(solution)/shard_map/reduce_scatter | solution.py:79
  112.0 116.2 %copy-start = (bf16[32,16,128]{2,1,0:T(8,128)(2,1)S(1)}, bf16[32,16,128]{2,1,0:T(8,128)(2,1)}, u32[]{:S(2)}) copy-start(bf16[32,16,128]{2,1,0:T(8,128)(2,1)} %param.5) | copy-start | bytes 393220
  112.0 116.2 %copy-start.3 = (bf16[2,128,128]{2,1,0:T(8,128)(2,1)S(1)}, bf16[2,128,128]{2,1,0:T(8,128)(2,1)}, u32[]{:S(2)}) copy-start(bf16[2,128,128]{2,1,0:T(8,128)(2,1)} %param.8) | copy-start | bytes 196612
  228.1 42.4 %copy-start.2 = (bf16[2,128,128]{2,1,0:T(8,128)(2,1)S(1)}, bf16[2,128,128]{2,1,0:T(8,128)(2,1)}, u32[]{:S(2)}) copy-start(bf16[2,128,128]{2,1,0:T(8,128)(2,1)} %param.9) | copy-start | bytes 196612
  228.1 109.0 %all-gather.9.cloned.1.call-start = ((), (), s32[]{:S(2)}) async-start(), calls=%async_computation.5 | async-start | bytes 2228224 | tf_op jit(solution)/shard_map/all_gather | solution.py:85
  228.6 42.8 %copy-start.1 = (bf16[2,128,512]{2,1,0:T(8,128)(2,1)S(1)}, bf16[2,128,512]{2,1,0:T(8,128)(2,1)}, u32[]{:S(2)}) copy-start(bf16[2,128,512]{2,1,0:T(8,128)(2,1)} %param.7) | copy-start | bytes 786436
  272.6 144.5 %all-gather.11.cloned.1.call-start = ((), (), s32[]{:S(2)}) async-start(), calls=%async_computation.6 | async-start | bytes 6291456 | tf_op jit(solution)/shard_map/all_gather | solution.py:88
  342.1 142.1 %all-gather.7.cloned.1.call-start = ((), (), s32[]{:S(2)}) async-start(), calls=%async_computation.4 | async-start | bytes 2228224 | tf_op jit(solution)/shard_map/all_gather | solution.py:86
  342.8 207.5 %all-reduce.5.cloned.1.call-start = ((), (), s32[]{:S(2)}) async-start(), calls=%async_computation.7 | async-start | bytes 8388608 | tf_op jit(solution)/shard_map/psum | solution.py:36
Sparse Core Ops, SparseCore 0:
  48.9 47.8 all-gather.4
  419.5 130.8 all-reduce.4
Sparse Core Ops, SparseCore 1:
  76.8 144.8 all-reduce.2
  228.2 38.1 reduce-scatter.1
  272.7 64.3 all-gather.8
  342.1 74.9 all-gather.10
  419.2 64.9 all-gather.6
